TPU v7x, 128 devices: a whole 4x4x4 slice. The times are simulated.
128 devices in a mesh: seq: 16 (over x_hi, y, core), head: 8 (over x_lo, z).
Axes of the slice: x: 4 (x_hi: 2, x_lo: 2; x = x_hi * 2 + x_lo), y: 4, z: 4, core: 2. Of those that a mesh axis runs over, the one named last changes fastest.
Arguments:
- tokens: bfloat16 [4096, 2048], P('seq'), may hold values from -6 to 6
- norm_gain: float32 [2048], replicated, may hold values from 0.1 to 1.9
- w_query: bfloat16 [2048, 4096], P(None, 'head')
- w_key: bfloat16 [2048, 512], replicated
- w_value: bfloat16 [2048, 512], replicated, may hold values from -0.125 to 0.125
- query_gain: float32 [128], replicated, may hold values from 0.5 to 5.5
- key_gain: float32 [128], replicated, may hold values from 0.5 to 5.5
- w_out: bfloat16 [4096, 2048], P('head'), may hold values from -0.5 to 0.5
- post_gain: float32 [2048], replicated, may hold values from 0.1 to 1.9
- doc_lengths: int32 [6], replicated, may hold values from 1 to 2560, 4096 in all
- expert_ids: int32 [4096, 8], P(('seq', 'head')), may hold values from 0 to 127, all different within a row; in each aligned block of 32 rows (0 to 31, 32 to 63, ...) at most 4 rows name the same one
- route_weights: float32 [4096, 8], P(('seq', 'head')), may hold values from 0.15 to 1
- w_gate: bfloat16 [128, 2048, 768], P(('seq', 'head')), may hold values from -0.125 to 0.125
- w_up: bfloat16 [128, 2048, 768], P(('seq', 'head')), may hold values from -0.125 to 0.125
- w_down: bfloat16 [128, 768, 2048], P(('seq', 'head')), may hold values from -0.21875 to 0.21875
Outputs:
- layer_out: bfloat16 [4096, 2048], P(('seq', 'head'))
Inputs may be any that keep to these rules, and one draw needn't show every extreme that they name: `doc_lengths`: 6 document lengths that sum to 4096; the largest is exactly 2560. `expert_ids`: each row names 8 different experts. Among the 32 rows of one device no expert is named more than 4 times; in some devices' rows some expert is named exactly 4 times.
All inputs are finite; a program needn't handle non-finite values.
Results may differ from a plain program's by a relative error of at most 0.015.
The roundings to bfloat16 on the way count: a program that leaves them out, or rounds other values in their place, can miss the bound.
Values may be sent and summed in bfloat16 or wider, within the bound.
No kernel may reach another device: no remote copies, remote signals or barrier semaphores. Data moves between devices by JAX's collectives and lax.ppermute only.
A program may use at most 128 MiB of HBM per device.

v0:
```python
import math
import jax
import jax.numpy as jnp
from jax import lax
from jax.sharding import PartitionSpec as P

HEADS = 32
KV_HEADS = 4
TOP = 8
EPSILON = 1e-06
THETA = 1000000.0
FLOOR = -1e30


def rms_scale(values, gain):
    return values * lax.rsqrt(jnp.mean(values * values, axis=-1, keepdims=True) + EPSILON) * gain


def rotate(values, cosine, sine):
    half = values.shape[-1] // 2
    first = values[..., :half]
    second = values[..., half:]
    return jnp.concatenate(
        [first * cosine - second * sine, second * cosine + first * sine], axis=-1
    )


def doc_index(positions, ends):
    return jnp.sum((positions[:, None] >= ends[None, :]).astype(jnp.int32), axis=1)


def local(
    tokens,
    norm_gain,
    w_query,
    w_key,
    w_value,
    query_gain,
    key_gain,
    w_out,
    post_gain,
    doc_lengths,
    expert_ids,
    route_weights,
    w_gate,
    w_up,
    w_down,
):
    tok_dev, width = tokens.shape
    head_dim = query_gain.shape[0]
    per_dev = w_query.shape[1] // head_dim
    n_seq = lax.axis_size("seq")
    n_head = lax.axis_size("head")
    seq_index = lax.axis_index("seq")
    head_index = lax.axis_index("head")
    ndocs = doc_lengths.shape[0]
    ends = jnp.cumsum(doc_lengths)
    starts = ends - doc_lengths
    positions = seq_index * tok_dev + jnp.arange(tok_dev, dtype=jnp.int32)
    query_doc = doc_index(positions, ends)
    matches = query_doc[:, None] == jnp.arange(ndocs, dtype=jnp.int32)[None, :]
    own_start = jnp.sum(jnp.where(matches, starts[None, :], 0), axis=1)
    offset = (positions - own_start).astype(jnp.float32)
    half = head_dim // 2
    inverse = THETA ** (-2.0 * jnp.arange(half, dtype=jnp.float32) / head_dim)
    angles = offset[:, None] * inverse[None, :]
    cosine = jnp.cos(angles)
    sine = jnp.sin(angles)
    inputs = tokens.astype(jnp.float32)
    normed = rms_scale(inputs, norm_gain).astype(jnp.bfloat16)
    queries = jnp.dot(normed, w_query, preferred_element_type=jnp.float32).reshape(
        tok_dev, per_dev, head_dim
    )
    queries = rotate(rms_scale(queries, query_gain), cosine[:, None, :], sine[:, None, :]).astype(
        jnp.bfloat16
    )
    column = head_index * per_dev // (HEADS // KV_HEADS) * head_dim
    key_cols = lax.dynamic_slice_in_dim(w_key, column, head_dim, 1)
    value_cols = lax.dynamic_slice_in_dim(w_value, column, head_dim, 1)
    keys = rotate(
        rms_scale(jnp.dot(normed, key_cols, preferred_element_type=jnp.float32), key_gain),
        cosine,
        sine,
    ).astype(jnp.bfloat16)
    values = jnp.dot(normed, value_cols, preferred_element_type=jnp.float32).astype(jnp.bfloat16)
    stacked = jnp.stack([keys, values])
    scale = head_dim ** (-0.5)
    last_query = positions[-1]
    first_start = own_start[0]

    def attend(state, block, key_start):
        count = block.shape[1]
        key_pos = key_start + jnp.arange(count, dtype=jnp.int32)

        def update(carry):
            high, total, accum = carry
            key_doc = doc_index(key_pos, ends)
            allowed = (
                (key_doc[None, :] == query_doc[:, None])
                & (key_pos[None, :] <= positions[:, None])
                & (key_pos[None, :] >= 0)
            )
            scores = (
                jnp.einsum("qhd,kd->hqk", queries, block[0], preferred_element_type=jnp.float32)
                * scale
            )
            scores = jnp.where(allowed[None], scores, FLOOR)
            new_high = jnp.maximum(high, jnp.max(scores, axis=2))
            weights = jnp.where(allowed[None], jnp.exp(scores - new_high[:, :, None]), 0.0)
            factor = jnp.exp(high - new_high)
            total = total * factor + jnp.sum(weights, axis=2)
            accum = accum * jnp.transpose(factor)[:, :, None] + jnp.einsum(
                "hqk,kd->qhd",
                weights.astype(jnp.bfloat16),
                block[1],
                preferred_element_type=jnp.float32,
            )
            return (new_high, total, accum)

        needed = (key_start <= last_query) & (key_start + count - 1 >= first_start)
        return lax.cond(needed, update, lambda carry: carry, state)

    initial = (
        jnp.full((per_dev, tok_dev), FLOOR, jnp.float32),
        jnp.zeros((per_dev, tok_dev), jnp.float32),
        jnp.zeros((tok_dev, per_dev, head_dim), jnp.float32),
    )
    piece = lax.all_gather(stacked, "seq", axis=1, tiled=True)
    count = piece.shape[1]
    step = math.gcd(count, tok_dev * max(1, 512 // tok_dev))

    def inner(index, carry):
        block = lax.dynamic_slice_in_dim(piece, index * step, step, 1)
        return attend(carry, block, index * step)

    state = lax.fori_loop(0, count // step, inner, initial)
    high, total, accum = state
    attended = (
        (accum / jnp.transpose(total)[:, :, None])
        .astype(jnp.bfloat16)
        .reshape(tok_dev, per_dev * head_dim)
    )
    rows = tok_dev // n_head
    attn_rows = lax.psum_scatter(
        jnp.dot(attended, w_out, preferred_element_type=jnp.float32).astype(jnp.bfloat16),
        "head",
        scatter_dimension=0,
        tiled=True,
    ).astype(jnp.float32)
    resid = lax.dynamic_slice_in_dim(inputs, head_index * rows, rows, 0) + attn_rows
    routed = rms_scale(resid, post_gain).astype(jnp.bfloat16)
    experts = n_seq * n_head * w_gate.shape[0]
    capacity = 2 * TOP * rows // experts
    chosen = expert_ids.reshape(-1)
    hits = (chosen[:, None] == jnp.arange(experts, dtype=jnp.int32)[None, :]).astype(jnp.int32)
    rank = jnp.sum((jnp.cumsum(hits, axis=0) - hits) * hits, axis=1)
    target = chosen * capacity + rank
    outgoing = (
        jnp.zeros((experts * capacity, width), jnp.bfloat16)
        .at[target]
        .set(jnp.repeat(routed, TOP, axis=0))
    )
    outgoing = outgoing.reshape(experts, capacity, width)
    block = lax.all_to_all(outgoing, ("seq", "head"), split_axis=0, concat_axis=0, tiled=True)
    flat = block.reshape(-1, width)
    gate = jnp.dot(flat, w_gate[0], preferred_element_type=jnp.float32)
    up = jnp.dot(flat, w_up[0], preferred_element_type=jnp.float32)
    hidden = (jax.nn.silu(gate) * up).astype(jnp.bfloat16)
    returned = lax.all_to_all(
        jnp.dot(hidden, w_down[0], preferred_element_type=jnp.float32)
        .astype(jnp.bfloat16)
        .reshape(block.shape),
        ("seq", "head"),
        split_axis=0,
        concat_axis=0,
        tiled=True,
    )
    picked = returned.reshape(experts * capacity, width)[target].reshape(rows, TOP, width)
    combined = jnp.sum(picked.astype(jnp.float32) * route_weights[:, :, None], axis=1)
    return (resid + combined).astype(jnp.bfloat16)


def solution(mesh):
    placed = (
        P("seq", None),
        P(),
        P(None, "head"),
        P(),
        P(),
        P(),
        P(),
        P("head", None),
        P(),
        P(),
        P(("seq", "head"), None),
        P(("seq", "head"), None),
        P(("seq", "head"), None, None),
        P(("seq", "head"), None, None),
        P(("seq", "head"), None, None),
    )
    return jax.shard_map(
        local, mesh=mesh, in_specs=placed, out_specs=P(("seq", "head"), None), check_vma=False
    )
```

profile of v0, /device:TPU:0, one launch (start us, length us, event | category | flops | bytes accessed | tf_op | source)
XLA Modules:
  0.0 291.0 jit_solution(13176573164525477628)
XLA Ops:
  6.6 1.7 multiply_reduce_fusion
  8.3 2.0 multiply_reduce_fusion.3
  10.3 0.7 reduce-window.18
  11.0 0.7 bitcast_subtract_fusion.1
  11.7 0.7 convert_reduce_fusion.1
  12.4 0.1 select_reduce_fusion
  12.5 0.5 copy-done.3
  13.0 1.9 fusion.30
  15.0 0.1 multiply_multiply_fusion
  15.0 0.3 multiply_cosine_fusion
  15.4 0.7 pad_maximum_fusion.1
  16.0 0.0 all-gather.2.cloned.1.call-update
  16.1 0.0 reduce-scatter.2.cloned.1.call-start
  16.1 0.6 slice.35
  16.7 0.6 slice.34
  17.3 0.1 copy.68
  17.3 0.1 copy.69
  17.5 3.5 %fusion.51 = f32[256,512]{1,0:T(8,128)} fusion(bf16[2048,512]{1,0:T(8,128)(2,1)} %param.21, f32[2048]{0:T(1024)S(1)} %copy-done.9, f32[256]{0:T(256)S(1)} %add_rsqrt_fusion.2, bf16[256,2048]{1,0:T(8,128)(2,1)} %param.19), kind=kOutput, calls=%fused_computation.99 | convolution fusion | flops 538968064 | bytes 3679232 | tf_op jit(solution)/shard_map/dot_general | solution.py:71
  20.9 2.0 reshape.304
  23.0 1.4 multiply_reduce_fusion.1
  24.4 0.1 copy.66
  24.5 1.2 fusion.36
  25.7 0.3 subtract_convert_fusion
  26.0 0.1 pad_maximum_fusion
  26.1 39.4 %all-gather.2.cloned.1.call-done = bf16[2,4096,128]{1,2,0:T(8,128)(2,1)} async-done(((bf16[2,256,128]{1,2,0:T(8,128)(2,1)}), bf16[2,4096,128]{1,2,0:T(8,128)(2,1)}) %all-gather.2.cloned.1.call-update) | async-done | bytes 2097168 | tf_op jit(solution)/shard_map/all_gather | solution.py:128
  65.6 4.1 %copy.70 = bf16[2,4096,128]{2,1,0:T(8,128)(2,1)} copy(bf16[2,4096,128]{1,2,0:T(8,128)(2,1)} %all-gather.2.cloned.1.call-done) | data formatting | bytes 4194304
  69.7 0.8 broadcast_in_dim.60
  70.5 18.4 %while.22 = (s32[]{:T(128)}, f32[4,256]{1,0:T(4,128)S(1)}, f32[4,256]{1,0:T(4,128)S(1)}, f32[256,4,128]{2,0,1:T(8,128)}, s32[]{:T(128)}, /*index=5*/s32[]{:T(128...) while((s32[]{:T(128)}, f32[4,256]{1,0:T(4,128)S(1)}, ...), condition=%wide.region_12.13_spmd.clone, body=%wide.region_6.12_spmd.clone.sunk | while | flops 276050688 | bytes 16863676 | solution.py:136
  71.7 8.4 %conditional.3 = ((f32[4,256]{1,0:T(4,128)S(1)}, f32[4,256]{1,0:T(4,128)S(1)}, f32[256,4,128]{2,0,1:T(8,128)})) conditional(s32[]{:T(128)} %convert_element_type.143, (f32[4,256]{1,0:T(4,128)S(1)}, f32[4,256]{1,0:T(4,128)S(1)}, f32[256,4,128]{2,0,1:T(8,128)}) %tuple.83, (s32[]{:T(128)}, s32[512]{0:T(512)S(1)}, s32[6]{0:T(128)}, s32[256]{0:T(256)}, ...), branch_computations={%region_7.7_spmd, %region_8.11_spmd} | conditional | flops 276050688 | bytes 16860310 | solution.py:121
  71.7 0.7 convert_reduce_fusion
  72.5 0.9 and_and_fusion
  73.4 2.7 fusion.2
  76.1 3.5 %fusion.5 = f32[256,4,128]{2,0,1:T(8,128)} fusion(f32[512,256,4]{1,0,2:T(8,128)} %get-tuple-element.592, f32[4,256]{1,0:T(4,128)S(1)} %get-tuple-element.679, pred[256,512]{0,1:T(8,128)(4,1)S(1)} %and_and_fusion, f32[256,4,128]{2,0,1:T(8,128)} %get-tuple-element.459, f32[256,4]{0,1:T(4,128)S(1)} %get-tuple-element.587, ...), kind=kOutput, calls=%fused_computation.9 | convolution fusion | flops 137101312 | bytes 3416072 | tf_op jit(solution)/shard_map/while/body/eval_jaxpr/cond/branch_1_fun/hqk,kd->qhd/dot_general | solution.py:112
  79.6 0.5 fusion.4
  88.9 2.0 copy.71
  91.0 1.1 divide_convert_fusion
  92.1 3.3 %convolution_convert_fusion = bf16[256,2048]{1,0:T(8,128)(2,1)} fusion(bf16[256,512]{0,1:T(8,128)(2,1)S(1)} %bitcast.89, bf16[512,2048]{1,0:T(8,128)(2,1)} %param.26), kind=kOutput, calls=%fused_computation.37 | convolution fusion | flops 537395200 | bytes 3407872 | tf_op jit(solution)/shard_map/dot_general | solution.py:145
  95.4 0.0 reduce-scatter.2.cloned.1.call-update
  95.4 2.8 convert_element_type.85
  98.2 0.1 copy.73
  98.3 0.1 eq.64
  98.4 0.1 eq.60
  98.5 0.1 copy.75
  98.6 0.2 fusion.41
  98.9 0.1 copy.72
  99.0 0.1 mul.258
  99.1 0.2 fusion.43
  99.3 66.3 %reduce-scatter.2.cloned.1.call-done = bf16[32,2048]{1,0:T(8,128)(2,1)} async-done(((bf16[256,2048]{1,0:T(8,128)(2,1)}), bf16[32,2048]{1,0:T(8,128)(2,1)}) %reduce-scatter.2.cloned.1.call-update) | async-done | bytes 131088 | tf_op jit(solution)/shard_map/reduce_scatter | solution.py:144
  165.6 1.2 multiply_reduce_fusion.2
  166.8 1.1 multiply_convert_fusion.2
  167.9 3.7 %scatter_custom_fusion = bf16[512,2048]{1,0:T(8,128)(2,1)} fusion(s32[256]{0:T(256)S(1)} %bitcast.95, bf16[]{:T(256)} %constant.154.clone.1, bf16[32,2048]{1,0:T(8,128)(2,1)S(1)} %multiply_convert_fusion.2), kind=kCustom, calls=%fused_computation.45 | custom fusion | bytes 2228226 | tf_op jit(solution)/shard_map/scatter | solution.py:161
  171.6 4.1 %reshape.308 = bf16[128,4,2048]{2,1,0:T(4,128)(2,1)} reshape(bf16[512,2048]{1,0:T(8,128)(2,1)} %scatter_custom_fusion) | data formatting | bytes 4194304 | tf_op jit(solution)/shard_map/reshape | solution.py:163
  175.7 37.7 %all_to_all.10 = bf16[128,4,2048]{2,1,0:T(4,128)(2,1)} all-to-all(bf16[128,4,2048]{2,1,0:T(4,128)(2,1)} %reshape.308), channel_id=1, replica_groups=mesh['seq'=16,'head'=8] {'seq','head'}, dimensions={0} | all-to-all | bytes 4194304 | tf_op jit(solution)/shard_map/all_to_all | solution.py:164
  213.5 4.0 %reshape.309 = bf16[512,2048]{1,0:T(8,128)(2,1)} reshape(bf16[128,4,2048]{2,1,0:T(4,128)(2,1)} %all_to_all.10) | data formatting | bytes 4194304 | tf_op jit(solution)/shard_map/reshape | solution.py:165
  217.4 5.5 %fusion.22 = f32[512,768]{1,0:T(8,128)} fusion(bf16[512,2048]{1,0:T(8,128)(2,1)} %reshape.309, bf16[1,2048,768]{2,1,0:T(8,128)(2,1)} %param.31), kind=kOutput, calls=%fused_computation.34 | convolution fusion | flops 1610612736 | bytes 6815744 | tf_op jit(solution)/shard_map/dot_general | solution.py:166
  222.9 8.3 %fusion.24 = bf16[512,2048]{1,0:T(8,128)(2,1)} fusion(bf16[1,768,2048]{2,1,0:T(8,128)(2,1)S(1)} %copy-done, f32[512,768]{1,0:T(8,128)} %fusion.22, bf16[512,2048]{1,0:T(8,128)(2,1)} %reshape.309, bf16[1,2048,768]{2,1,0:T(8,128)(2,1)} %param.32), kind=kOutput, calls=%fused_computation.36 | convolution fusion | flops 3224633344 | bytes 12058624 | tf_op jit(solution)/shard_map/dot_general | solution.py:170
  231.2 4.1 %reshape.310 = bf16[128,4,2048]{2,1,0:T(4,128)(2,1)} reshape(bf16[512,2048]{1,0:T(8,128)(2,1)} %fusion.24) | data formatting | bytes 4194304 | tf_op jit(solution)/shard_map/reshape | solution.py:172
  235.3 5.9 %all-to-all-start.1 = ((bf16[128,4,2048]{2,1,0:T(4,128)(2,1)}), bf16[128,4,2048]{2,1,0:T(4,128)(2,1)}, u32[]{:S(2)}, u32[]{:S(2)}) async-start(bf16[128,4,2048]{2,1,0:T(4,128)(2,1)} %reshape.310), calls=%async_computation.2 | async-start | bytes 4194304 | tf_op jit(solution)/shard_map/all_to_all | solution.py:169
  241.2 0.1 copy.77
  241.3 29.7 %all-to-all-done.1 = bf16[128,4,2048]{2,1,0:T(4,128)(2,1)} async-done(((bf16[128,4,2048]{2,1,0:T(4,128)(2,1)}), bf16[128,4,2048]{2,1,0:T(4,128)(2,1)}, u32[]{:S(2)}, u32[]{:S(2)}) %all-to-all-start.1) | async-done | bytes 2097184 | tf_op jit(solution)/shard_map/all_to_all | solution.py:169
  271.0 4.0 %reshape.311 = bf16[512,2048]{1,0:T(8,128)(2,1)} reshape(bf16[128,4,2048]{2,1,0:T(4,128)(2,1)} %all-to-all-done.1) | data formatting | bytes 4194304 | tf_op jit(solution)/shard_map/reshape | solution.py:178
  275.0 5.2 %gather_fusion = bf16[256,2048]{1,0:T(8,128)(2,1)} fusion(bf16[512,2048]{1,0:T(8,128)(2,1)} %reshape.311, s32[1024]{0:T(1024)S(1)} %pad_clamp_fusion), kind=kCustom, calls=%fused_computation | custom fusion | bytes 2098176 | tf_op jit(solution)/shard_map/gather | solution.py:178
  280.2 2.2 fusion.27
  282.5 1.7 add_convert_fusion.1
  (68 shorter events, 0.4 us)
Async XLA Ops:
  6.5 216.4 %copy-start = (bf16[1,768,2048]{2,1,0:T(8,128)(2,1)S(1)}, bf16[1,768,2048]{2,1,0:T(8,128)(2,1)}, u32[]{:S(2)}) copy-start(bf16[1,768,2048]{2,1,0:T(8,128)(2,1)} %param.33) | copy-start | bytes 9437188
  6.5 6.5 %copy-start.9 = (f32[2048]{0:T(1024)S(1)}, f32[2048]{0:T(1024)}, u32[]{:S(2)}) copy-start(f32[2048]{0:T(1024)} %param.20) | copy-start | bytes 24580
  6.5 3.7 %copy-start.10 = (s32[6]{0:T(128)S(1)}, s32[6]{0:T(128)}, u32[]{:S(2)}) copy-start(s32[6]{0:T(128)} %param.28) | copy-start | bytes 76
  6.5 59.0 %all-gather.2.cloned.1.call-start = ((), (), s32[]{:S(2)}) async-start(), calls=%async_computation.3 | async-start | bytes 2228224 | tf_op jit(solution)/shard_map/all_gather | solution.py:128
  8.3 6.7 %copy-start.7 = (f32[128]{0:T(128)S(1)}, f32[128]{0:T(128)}, u32[]{:S(2)}) copy-start(f32[128]{0:T(128)} %param.25) | copy-start | bytes 1540
  12.4 0.6 copy-start.3
  16.1 149.5 %reduce-scatter.2.cloned.1.call-start = ((), (), s32[]{:S(2)}) async-start(), calls=%async_computation.4 | async-start | bytes 1179648 | tf_op jit(solution)/shard_map/reduce_scatter | solution.py:144
  17.4 7.0 %copy-start.8 = (f32[128]{0:T(128)S(1)}, f32[128]{0:T(128)}, u32[]{:S(2)}) copy-start(f32[128]{0:T(128)} %param.24) | copy-start | bytes 1540
  76.1 3.5 %copy-start.1 = (f32[512,256,4]{1,0,2:T(8,128)S(1)}, f32[512,256,4]{1,0,2:T(8,128)}, u32[]{:S(2)}) copy-start(f32[512,256,4]{1,0,2:T(8,128)} %get-tuple-element.592) | copy-start | bytes 6291460 | tf_op jit(solution)/shard_map/while/body/eval_jaxpr/cond
  95.4 2.9 copy-start.4
  95.4 71.4 %copy-start.5 = (f32[2048]{0:T(1024)S(1)}, f32[2048]{0:T(1024)}, u32[]{:S(2)}) copy-start(f32[2048]{0:T(1024)} %param.27) | copy-start | bytes 24580
  235.3 5.9 %copy-start.6 = (f32[32,8]{0,1:T(8,128)S(1)}, f32[32,8]{0,1:T(8,128)}, u32[]{:S(2)}) copy-start(f32[32,8]{0,1:T(8,128)} %param.30) | copy-start | bytes 3076
  235.3 35.7 %all-to-all-start.1 = ((bf16[128,4,2048]{2,1,0:T(4,128)(2,1)}), bf16[128,4,2048]{2,1,0:T(4,128)(2,1)}, u32[]{:S(2)}, u32[]{:S(2)}) async-start(bf16[128,4,2048]{2,1,0:T(4,128)(2,1)} %reshape.310), calls=%async_computation.2 | async-start | bytes 4194304 | tf_op jit(solution)/shard_map/all_to_all | solution.py:169
  275.0 7.5 %copy-start.2 = (bf16[32,2048]{1,0:T(8,128)(2,1)S(1)}, bf16[32,2048]{1,0:T(8,128)(2,1)}, u32[]{:S(2)}) copy-start(bf16[32,2048]{1,0:T(8,128)(2,1)} %reduce-scatter.2.cloned.1.call-done) | copy-start | bytes 393220
Sparse Core Ops, SparseCore 0:
  16.2 49.3 all-gather.1
  95.5 70.0 reduce-scatter.1
where the time goes:
time: 292 us; the launch traced here: 291 us
  waiting for transfers between devices  135 us (46%)
  blocking collectives  37.7 us (13%)
  local copies, waits for them, and re-layouts  36.7 us (13%)
  matrix products  30.5 us (10%)
  other arithmetic  20.8 us (7%)
  between operations  13.7 us (5%)
  loops' own time  10 us (3%)
  starting transfers between devices  5.95 us (2%)
    reduce_scatter x1, waiting for transfers between devices, local(): lax.psum_scatter(jnp.dot(attended, w_out, preferred_element_type=jnp.floa...  66.3 us
    all_gather x1, waiting for transfers between devices, local(): piece = lax.all_gather(stacked, 'seq', axis=1, tiled=True)  39.4 us
    all_to_all x1, blocking collectives, local(): lax.all_to_all(outgoing, ('seq', 'head'), split_axis=0, concat_axis=0, ti...  37.7 us
    all_to_all x1, waiting for transfers between devices, local(): lax.all_to_all(jnp.dot(hidden, w_down[0], preferred_element_type=jnp.floa...  29.7 us
    another operation x1, loops' own time, local(): state = lax.fori_loop(0, count // step, inner, initial)  9.87 us
    dot_general x1, matrix products, local(): jnp.dot(hidden, w_down[0], preferred_element_type=jnp.float32)  8.26 us
    all_to_all x1, starting transfers between devices, local(): lax.all_to_all(jnp.dot(hidden, w_down[0], preferred_element_type=jnp.floa...  5.91 us
  transfers between devices with their start and end apart: 3, of which 3 were waited for; matrix products, arithmetic and copies ran while one was open for 5% of the time, Pallas kernels for 0%

commit v1 on v0

--- a/solution.py
+++ b/solution.py
@@ -3,6 +3,7 @@
 import jax.numpy as jnp
 from jax import lax
 from jax.sharding import PartitionSpec as P
+from jax.lax import all_to_all, axis_size
 
 HEADS = 32
 KV_HEADS = 4
@@ -125,7 +126,9 @@
         jnp.zeros((per_dev, tok_dev), jnp.float32),
         jnp.zeros((tok_dev, per_dev, head_dim), jnp.float32),
     )
-    piece = lax.all_gather(stacked, "seq", axis=1, tiled=True)
+    piece = jnp.concatenate(
+        all_to_all(jnp.stack(axis_size("seq") * [stacked], axis=0), "seq", 0, 0), axis=1
+    )
     count = piece.shape[1]
     step = math.gcd(count, tok_dev * max(1, 512 // tok_dev))
 

time: 292 us -> 281 us (0.962)
  waiting for transfers between devices: 135 us -> 116 us
  starting transfers between devices: 5.95 us -> 13.1 us
    all_gather x1 -> x0, waiting for transfers between devices: 39.4 us -> none  [local(): piece = lax.all_gather(stacked, 'seq', axis=1, tiled=True)]
    all_to_all x0 -> x1, waiting for transfers between devices: none -> 19.2 us  [local(): all_to_all(jnp.stack(axis_size('seq') * [stacked], axis=0), 'seq', 0, 0)]
    all_to_all x0 -> x1, starting transfers between devices: none -> 7.16 us  [local(): all_to_all(jnp.stack(axis_size('seq') * [stacked], axis=0), 'seq', 0, 0)]
    unnamed x24 -> x23, local copies, waits for them, and re-layouts: 4.77 us -> 0.67 us
    all_to_all x0 -> x1, local copies, waits for them, and re-layouts: none -> 3.17 us  [local(): all_to_all(jnp.stack(axis_size('seq') * [stacked], axis=0), 'seq', 0, 0)]
where the time goes in v1:
time: 281 us; the launch traced here: 280 us
  waiting for transfers between devices  116 us (41%)
  local copies, waits for them, and re-layouts  37.8 us (13%)
  blocking collectives  37.7 us (13%)
  matrix products  30.6 us (11%)
  other arithmetic  20.2 us (7%)
  between operations  13.7 us (5%)
  starting transfers between devices  13.1 us (5%)
  loops' own time  10.6 us (4%)
    reduce_scatter x1, waiting for transfers between devices, local(): lax.psum_scatter(jnp.dot(attended, w_out, preferred_element_type=jnp.floa...  67.4 us
    all_to_all x1, blocking collectives, local(): lax.all_to_all(outgoing, ('seq', 'head'), split_axis=0, concat_axis=0, ti...  37.7 us
    all_to_all x1, waiting for transfers between devices, local(): lax.all_to_all(jnp.dot(hidden, w_down[0], preferred_element_type=jnp.floa...  29.7 us
    all_to_all x1, waiting for transfers between devices, local(): all_to_all(jnp.stack(axis_size('seq') * [stacked], axis=0), 'seq', 0, 0)  19.2 us
    another operation x1, loops' own time, local(): state = lax.fori_loop(0, count // step, inner, initial)  10.4 us
    dot_general x1, matrix products, local(): jnp.dot(hidden, w_down[0], preferred_element_type=jnp.float32)  8.26 us
    all_to_all x1, starting transfers between devices, local(): all_to_all(jnp.stack(axis_size('seq') * [stacked], axis=0), 'seq', 0, 0)  7.16 us
    all_to_all x1, starting transfers between devices, local(): lax.all_to_all(jnp.dot(hidden, w_down[0], preferred_element_type=jnp.floa...  5.91 us
  transfers between devices with their start and end apart: 3, of which 3 were waited for; matrix products, arithmetic and copies ran while one was open for 5% of the time, Pallas kernels for 0%

profile of v1, /device:TPU:0, one launch (start us, length us, event | category | flops | bytes accessed | tf_op | source)
XLA Modules:
  0.0 280.0 jit_solution(12020925077879993320)
XLA Ops:
  6.6 1.7 multiply_reduce_fusion
  8.3 2.0 multiply_reduce_fusion.3
  10.3 0.8 reduce-window.18
  11.0 0.7 bitcast_subtract_fusion.1
  11.7 0.8 convert_reduce_fusion.1
  12.4 0.1 select_reduce_fusion
  12.5 0.5 copy-done.3
  13.0 1.9 fusion.30
  15.0 0.1 multiply_multiply_fusion
  15.0 0.3 multiply_cosine_fusion
  15.4 0.1 copy.82
  15.5 1.8 stack.8
  17.4 7.2 %all-to-all-start = ((bf16[16,2,256,128]{3,2,1,0:T(8,128)(2,1)}), bf16[16,2,256,128]{3,2,1,0:T(8,128)(2,1)}, u32[]{:S(2)}, u32[]{:S(2)}) async-start(bf16[16,2,256,128]{3,2,1,0:T(8,128)(2,1)} %stack.8), calls=%async_computation | async-start | bytes 4194304 | tf_op jit(solution)/shard_map/all_to_all | solution.py:130
  24.5 0.0 reduce-scatter.2.cloned.1.call-start
  24.6 0.5 slice.35
  25.1 0.7 slice.34
  25.7 0.1 copy.86
  25.8 0.1 copy.87
  25.9 3.5 %fusion.51 = f32[256,512]{1,0:T(8,128)} fusion(bf16[2048,512]{1,0:T(8,128)(2,1)} %param.21, f32[2048]{0:T(1024)} %param.20, f32[256]{0:T(256)S(1)} %add_rsqrt_fusion.2, bf16[256,2048]{1,0:T(8,128)(2,1)} %param.19), kind=kOutput, calls=%fused_computation.99 | convolution fusion | flops 538968064 | bytes 3679232 | tf_op jit(solution)/shard_map/dot_general | solution.py:72
  29.4 2.0 reshape.314
  31.5 1.4 multiply_reduce_fusion.1
  32.9 0.1 copy.84
  33.0 1.2 fusion.36
  34.2 0.3 subtract_convert_fusion
  34.5 0.1 pad_maximum_fusion
  34.6 19.2 %all-to-all-done = bf16[16,2,256,128]{3,2,1,0:T(8,128)(2,1)} async-done(((bf16[16,2,256,128]{3,2,1,0:T(8,128)(2,1)}), bf16[16,2,256,128]{3,2,1,0:T(8,128)(2,1)}, u32[]{:S(2)}, u32[]{:S(2)}) %all-to-all-start) | async-done | bytes 2097184 | tf_op jit(solution)/shard_map/all_to_all | solution.py:130
  53.9 3.2 %copy.83 = bf16[16,2,256,128]{3,2,0,1:T(8,128)(2,1)} copy(bf16[16,2,256,128]{3,2,1,0:T(8,128)(2,1)} %all-to-all-done) | data formatting | bytes 4194304 | tf_op jit(solution)/shard_map/all_to_all | solution.py:130
  57.0 0.8 broadcast_in_dim.60
  57.9 19.0 %while.22 = (s32[]{:T(128)}, f32[4,256]{1,0:T(4,128)S(1)}, f32[4,256]{1,0:T(4,128)S(1)}, f32[256,4,128]{2,0,1:T(8,128)}, s32[]{:T(128)}, /*index=5*/s32[]{:T(128...) while((s32[]{:T(128)}, f32[4,256]{1,0:T(4,128)S(1)}, ...), condition=%wide.region_12.13_spmd.clone, body=%wide.region_6.12_spmd.clone.sunk | while | flops 276050688 | bytes 16863676 | solution.py:139
  59.2 8.5 %conditional.3 = ((f32[4,256]{1,0:T(4,128)S(1)}, f32[4,256]{1,0:T(4,128)S(1)}, f32[256,4,128]{2,0,1:T(8,128)})) conditional(s32[]{:T(128)} %convert_element_type.143, (f32[4,256]{1,0:T(4,128)S(1)}, f32[4,256]{1,0:T(4,128)S(1)}, f32[256,4,128]{2,0,1:T(8,128)}) %tuple.78, (s32[]{:T(128)}, s32[512]{0:T(512)S(1)}, s32[6]{0:T(128)}, s32[256]{0:T(256)}, ...), branch_computations={%region_7.7_spmd, %region_8.11_spmd} | conditional | flops 276050688 | bytes 16860310 | solution.py:122
  59.2 0.8 convert_reduce_fusion
  59.9 0.9 and_and_fusion
  60.9 2.7 fusion.2
  63.6 3.5 %fusion.5 = f32[256,4,128]{2,0,1:T(8,128)} fusion(f32[512,256,4]{1,0,2:T(8,128)} %get-tuple-element.537, f32[4,256]{1,0:T(4,128)S(1)} %get-tuple-element.624, pred[256,512]{0,1:T(8,128)(4,1)S(1)} %and_and_fusion, f32[256,4,128]{2,0,1:T(8,128)} %get-tuple-element.459, f32[256,4]{0,1:T(4,128)S(1)} %get-tuple-element.532, ...), kind=kOutput, calls=%fused_computation.9 | convolution fusion | flops 137101312 | bytes 3416072 | tf_op jit(solution)/shard_map/while/body/eval_jaxpr/cond/branch_1_fun/hqk,kd->qhd/dot_general | solution.py:113
  67.1 0.5 fusion.4
  76.9 2.0 copy.88
  78.9 1.1 divide_convert_fusion
  80.0 3.3 %convolution_convert_fusion = bf16[256,2048]{1,0:T(8,128)(2,1)} fusion(bf16[256,512]{0,1:T(8,128)(2,1)S(1)} %bitcast.93, bf16[512,2048]{1,0:T(8,128)(2,1)} %param.26), kind=kOutput, calls=%fused_computation.37 | convolution fusion | flops 537395200 | bytes 3407872 | tf_op jit(solution)/shard_map/dot_general | solution.py:148
  83.4 2.8 %convert_element_type.85 = f32[256,2048]{1,0:T(8,128)} convert(bf16[256,2048]{1,0:T(8,128)(2,1)} %param.19) | non-fusion elementwise | flops 524288 | bytes 3145728 | tf_op jit(solution)/shard_map/convert_element_type | solution.py:70
  86.2 0.1 copy.90
  86.3 0.1 eq.64
  86.4 0.1 eq.60
  86.5 0.1 copy.92
  86.6 0.2 fusion.41
  86.9 0.1 copy.89
  87.0 0.1 mul.258
  87.1 0.2 fusion.43
  87.3 67.4 %reduce-scatter.2.cloned.1.call-done = bf16[32,2048]{1,0:T(8,128)(2,1)} async-done(((bf16[256,2048]{1,0:T(8,128)(2,1)}), bf16[32,2048]{1,0:T(8,128)(2,1)}) %reduce-scatter.2.cloned.1.call-update) | async-done | bytes 131088 | tf_op jit(solution)/shard_map/reduce_scatter | solution.py:147
  154.6 1.2 multiply_reduce_fusion.2
  155.8 1.1 multiply_convert_fusion.2
  157.0 3.7 %scatter_custom_fusion = bf16[512,2048]{1,0:T(8,128)(2,1)} fusion(s32[256]{0:T(256)S(1)} %bitcast.99, bf16[]{:T(256)} %constant.154.clone.1, bf16[32,2048]{1,0:T(8,128)(2,1)S(1)} %multiply_convert_fusion.2), kind=kCustom, calls=%fused_computation.45 | custom fusion | bytes 2228226 | tf_op jit(solution)/shard_map/scatter | solution.py:164
  160.7 4.1 %reshape.318 = bf16[128,4,2048]{2,1,0:T(4,128)(2,1)} reshape(bf16[512,2048]{1,0:T(8,128)(2,1)} %scatter_custom_fusion) | data formatting | bytes 4194304 | tf_op jit(solution)/shard_map/reshape | solution.py:166
  164.8 37.7 %all_to_all.15 = bf16[128,4,2048]{2,1,0:T(4,128)(2,1)} all-to-all(bf16[128,4,2048]{2,1,0:T(4,128)(2,1)} %reshape.318), channel_id=1, replica_groups=mesh['seq'=16,'head'=8] {'seq','head'}, dimensions={0} | all-to-all | bytes 4194304 | tf_op jit(solution)/shard_map/all_to_all | solution.py:167
  202.5 4.0 %reshape.319 = bf16[512,2048]{1,0:T(8,128)(2,1)} reshape(bf16[128,4,2048]{2,1,0:T(4,128)(2,1)} %all_to_all.15) | data formatting | bytes 4194304 | tf_op jit(solution)/shard_map/reshape | solution.py:168
  206.4 5.5 %fusion.22 = f32[512,768]{1,0:T(8,128)} fusion(bf16[512,2048]{1,0:T(8,128)(2,1)} %reshape.319, bf16[1,2048,768]{2,1,0:T(8,128)(2,1)} %param.31), kind=kOutput, calls=%fused_computation.34 | convolution fusion | flops 1610612736 | bytes 6815744 | tf_op jit(solution)/shard_map/dot_general | solution.py:169
  211.9 8.3 %fusion.24 = bf16[512,2048]{1,0:T(8,128)(2,1)} fusion(bf16[1,768,2048]{2,1,0:T(8,128)(2,1)S(1)} %copy-done, f32[512,768]{1,0:T(8,128)} %fusion.22, bf16[512,2048]{1,0:T(8,128)(2,1)} %reshape.319, bf16[1,2048,768]{2,1,0:T(8,128)(2,1)} %param.32), kind=kOutput, calls=%fused_computation.36 | convolution fusion | flops 3224633344 | bytes 12058624 | tf_op jit(solution)/shard_map/dot_general | solution.py:173
  220.2 4.1 %reshape.320 = bf16[128,4,2048]{2,1,0:T(4,128)(2,1)} reshape(bf16[512,2048]{1,0:T(8,128)(2,1)} %fusion.24) | data formatting | bytes 4194304 | tf_op jit(solution)/shard_map/reshape | solution.py:175
  224.3 5.9 %all-to-all-start.2 = ((bf16[128,4,2048]{2,1,0:T(4,128)(2,1)}), bf16[128,4,2048]{2,1,0:T(4,128)(2,1)}, u32[]{:S(2)}, u32[]{:S(2)}) async-start(bf16[128,4,2048]{2,1,0:T(4,128)(2,1)} %reshape.320), calls=%async_computation.3 | async-start | bytes 4194304 | tf_op jit(solution)/shard_map/all_to_all | solution.py:172
  230.2 0.1 copy.94
  230.3 29.7 %all-to-all-done.2 = bf16[128,4,2048]{2,1,0:T(4,128)(2,1)} async-done(((bf16[128,4,2048]{2,1,0:T(4,128)(2,1)}), bf16[128,4,2048]{2,1,0:T(4,128)(2,1)}, u32[]{:S(2)}, u32[]{:S(2)}) %all-to-all-start.2) | async-done | bytes 2097184 | tf_op jit(solution)/shard_map/all_to_all | solution.py:172
  260.0 4.0 %reshape.321 = bf16[512,2048]{1,0:T(8,128)(2,1)} reshape(bf16[128,4,2048]{2,1,0:T(4,128)(2,1)} %all-to-all-done.2) | data formatting | bytes 4194304 | tf_op jit(solution)/shard_map/reshape | solution.py:181
  264.0 5.2 %gather_fusion = bf16[256,2048]{1,0:T(8,128)(2,1)} fusion(bf16[512,2048]{1,0:T(8,128)(2,1)} %reshape.321, s32[1024]{0:T(1024)S(1)} %pad_clamp_fusion), kind=kCustom, calls=%fused_computation | custom fusion | bytes 2098176 | tf_op jit(solution)/shard_map/gather | solution.py:181
  269.2 2.2 fusion.27
  271.5 1.7 add_convert_fusion.1
  (69 shorter events, 0.4 us)
Async XLA Ops:
  6.5 205.4 %copy-start = (bf16[1,768,2048]{2,1,0:T(8,128)(2,1)S(1)}, bf16[1,768,2048]{2,1,0:T(8,128)(2,1)}, u32[]{:S(2)}) copy-start(bf16[1,768,2048]{2,1,0:T(8,128)(2,1)} %param.33) | copy-start | bytes 9437188
  6.5 6.5 %copy-start.9 = (f32[2048]{0:T(1024)S(1)}, f32[2048]{0:T(1024)}, u32[]{:S(2)}) copy-start(f32[2048]{0:T(1024)} %param.20) | copy-start | bytes 24580
  6.5 3.7 %copy-start.10 = (s32[6]{0:T(128)S(1)}, s32[6]{0:T(128)}, u32[]{:S(2)}) copy-start(s32[6]{0:T(128)} %param.28) | copy-start | bytes 76
  8.2 6.7 %copy-start.7 = (f32[128]{0:T(128)S(1)}, f32[128]{0:T(128)}, u32[]{:S(2)}) copy-start(f32[128]{0:T(128)} %param.25) | copy-start | bytes 1540
  12.4 0.6 copy-start.3
  17.4 36.5 %all-to-all-start = ((bf16[16,2,256,128]{3,2,1,0:T(8,128)(2,1)}), bf16[16,2,256,128]{3,2,1,0:T(8,128)(2,1)}, u32[]{:S(2)}, u32[]{:S(2)}) async-start(bf16[16,2,256,128]{3,2,1,0:T(8,128)(2,1)} %stack.8), calls=%async_computation | async-start | bytes 4194304 | tf_op jit(solution)/shard_map/all_to_all | solution.py:130
  24.5 130.1 %reduce-scatter.2.cloned.1.call-start = ((), (), s32[]{:S(2)}) async-start(), calls=%async_computation.4 | async-start | bytes 1179648 | tf_op jit(solution)/shard_map/reduce_scatter | solution.py:147
  25.9 7.0 %copy-start.8 = (f32[128]{0:T(128)S(1)}, f32[128]{0:T(128)}, u32[]{:S(2)}) copy-start(f32[128]{0:T(128)} %param.24) | copy-start | bytes 1540
  63.6 3.5 %copy-start.1 = (f32[512,256,4]{1,0,2:T(8,128)S(1)}, f32[512,256,4]{1,0,2:T(8,128)}, u32[]{:S(2)}) copy-start(f32[512,256,4]{1,0,2:T(8,128)} %get-tuple-element.537) | copy-start | bytes 6291460 | tf_op jit(solution)/shard_map/while/body/eval_jaxpr/cond
  83.3 2.9 %copy-start.4 = (s32[32,8]{0,1:T(8,128)S(1)}, s32[32,8]{0,1:T(8,128)}, u32[]{:S(2)}) copy-start(s32[32,8]{0,1:T(8,128)} %param.29) | copy-start | bytes 3076
  83.4 72.4 %copy-start.5 = (f32[2048]{0:T(1024)S(1)}, f32[2048]{0:T(1024)}, u32[]{:S(2)}) copy-start(f32[2048]{0:T(1024)} %param.27) | copy-start | bytes 24580
  224.3 5.9 %copy-start.6 = (f32[32,8]{0,1:T(8,128)S(1)}, f32[32,8]{0,1:T(8,128)}, u32[]{:S(2)}) copy-start(f32[32,8]{0,1:T(8,128)} %param.30) | copy-start | bytes 3076
  224.3 35.7 %all-to-all-start.2 = ((bf16[128,4,2048]{2,1,0:T(4,128)(2,1)}), bf16[128,4,2048]{2,1,0:T(4,128)(2,1)}, u32[]{:S(2)}, u32[]{:S(2)}) async-start(bf16[128,4,2048]{2,1,0:T(4,128)(2,1)} %reshape.320), calls=%async_computation.3 | async-start | bytes 4194304 | tf_op jit(solution)/shard_map/all_to_all | solution.py:172
  264.0 7.5 %copy-start.2 = (bf16[32,2048]{1,0:T(8,128)(2,1)S(1)}, bf16[32,2048]{1,0:T(8,128)(2,1)}, u32[]{:S(2)}) copy-start(bf16[32,2048]{1,0:T(8,128)(2,1)} %reduce-scatter.2.cloned.1.call-done) | copy-start | bytes 393220
Sparse Core Ops, SparseCore 0:
  83.5 71.1 reduce-scatter.1
